TPU v7x, 256 devices: a whole 4x4x8 slice. The times are simulated.
256 devices in a mesh: dp: 4 (over x), expert: 64 (over z, y, core).
Axes of the slice: x: 4, y: 4, z: 8, core: 2. Of those that a mesh axis runs over, the one named last changes fastest.
Arguments:
- tokens: bfloat16 [4096, 2048], P(('dp', 'expert')), may hold values from -6 to 6
- expert_ids: int32 [4096, 8], P(('dp', 'expert')), may hold values from 0 to 127, all different within a row; in each aligned block of 16 rows (0 to 15, 16 to 31, ...) at most 2 rows name the same one
- gate_weights: float32 [4096, 8], P(('dp', 'expert')), may hold values from 0.1 to 1
- hot_experts: int32 [2], replicated, may hold values from 0 to 127, as said below
- capacity: int32 [128], replicated, may hold values from 32 to 64
- w_in: bfloat16 [128, 2048, 1536], P('expert', None, 'dp'), may hold values from -0.125 to 0.125
- w_out: bfloat16 [128, 1536, 2048], P('expert', 'dp'), may hold values from -0.15625 to 0.15625
- grad_y: bfloat16 [4096, 2048], P(('dp', 'expert')), may hold values from -1.5 to 1.5
Outputs:
- mixed: bfloat16 [4096, 2048], P(('dp', 'expert'))
- token_grad: bfloat16 [4096, 2048], P(('dp', 'expert'))
- gate_grad: float32 [4096, 8], P(('dp', 'expert'))
- grad_w_in: bfloat16 [128, 2048, 1536], P('expert', None, 'dp')
- grad_w_out: bfloat16 [128, 1536, 2048], P('expert', 'dp')
Inputs may be any that keep to these rules, and one draw needn't show every extreme that they name: `expert_ids`: among the tokens of one device no expert is named more than 2 times, a bound that some block reaches. `hot_experts`: 2 different experts; the last entry is always expert 128 - 1.
All inputs are finite; a program needn't handle non-finite values.
Results may differ from a plain program's by a relative error of at most 0.012.
Values may be sent and summed in bfloat16 or wider, within the bound.
No kernel may reach another device: no remote copies, remote signals or barrier semaphores. Data moves between devices by JAX's collectives and lax.ppermute only.
A program may use at most 128 MiB of HBM per device.

v0:
```python
import jax
import jax.numpy as jnp
from jax import lax
from jax.sharding import PartitionSpec as P


def prefix(part, axis, combine, identity):
    place = lax.axis_index(axis)
    gathered = lax.all_gather(part, axis)
    state = jnp.zeros_like(part) + jnp.asarray(identity, part.dtype)

    def one(turn, state):
        return combine(state, lax.dynamic_index_in_dim(gathered, turn, 0, False))

    return lax.fori_loop(0, place, one, state)


def silu_terms(pre_act):
    sig_val = jax.nn.sigmoid(pre_act)
    return (pre_act * sig_val, sig_val * (1.0 + pre_act * (1.0 - sig_val)))


def expert_math(rows_x, rows_g, weight_in, weight_out):
    pre_act = jnp.einsum("gerd,edh->gerh", rows_x, weight_in, preferred_element_type=jnp.float32)
    act_full, slope_val = silu_terms(pre_act)
    act_low = act_full.astype(jnp.bfloat16)
    out_part = jnp.einsum("gerh,ehd->gerd", act_low, weight_out, preferred_element_type=jnp.float32)
    back_act = jnp.einsum("gerd,ehd->gerh", rows_g, weight_out, preferred_element_type=jnp.float32)
    pre_grad = (back_act * slope_val).astype(jnp.bfloat16)
    in_part = jnp.einsum("gerh,edh->gerd", pre_grad, weight_in, preferred_element_type=jnp.float32)
    grad_in = jnp.einsum("gerd,gerh->edh", rows_x, pre_grad, preferred_element_type=jnp.float32)
    grad_out = jnp.einsum("gerh,gerd->ehd", act_low, rows_g, preferred_element_type=jnp.float32)
    stacked = jnp.stack([out_part, in_part], axis=1)
    partial_terms = lax.optimization_barrier(stacked.astype(jnp.bfloat16)).astype(jnp.float32)
    return (partial_terms, grad_in, grad_out)


def local(tokens, expert_ids, gate_weights, hot_experts, capacity, w_in, w_out, grad_y):
    highest = lax.Precision.HIGHEST
    expert_devs = lax.axis_size("expert")
    tok_rows, top_k = expert_ids.shape
    local_experts = w_in.shape[0]
    expert_total = local_experts * expert_devs
    slot_count = max(2, 3 * tok_rows * top_k // (2 * expert_total))
    feature_dim = tokens.shape[1]
    labels = jnp.arange(expert_total, dtype=jnp.int32)
    name_hit = (expert_ids[:, :, None] == labels).astype(jnp.int32)
    per_token = jnp.sum(name_hit, axis=1)
    local_counts = jnp.sum(per_token, axis=0)
    earlier = prefix(
        local_counts, "expert", lambda first, second: first + second, jnp.zeros_like(local_counts)
    )
    within_dev = jnp.cumsum(per_token, axis=0) - per_token
    rank_of = earlier[None, :] + within_dev
    is_hot = jnp.any(labels[:, None] == hot_experts[None, :], axis=1)
    keep_mask = jnp.logical_or(is_hot[None, :], rank_of < capacity[None, :]).astype(jnp.float32)
    slot_hit = (within_dev[:, :, None] == jnp.arange(slot_count, dtype=jnp.int32)).astype(
        jnp.float32
    )
    chosen = name_hit.astype(jnp.float32) * keep_mask[:, None, :]
    pick_mask = chosen[:, :, :, None] * slot_hit[:, None, :, :]
    sending = jnp.ones((expert_total,), jnp.float32)
    send_picks = pick_mask * sending[None, None, :, None]
    rows_sel = jnp.sum(send_picks, axis=1)
    gate_sel = jnp.einsum("tkes,tk->tes", send_picks, gate_weights, precision=highest)
    grad_f32 = grad_y.astype(jnp.float32)
    x_buf = jnp.einsum(
        "tes,td->esd", rows_sel.astype(jnp.bfloat16), tokens, preferred_element_type=jnp.float32
    ).astype(jnp.bfloat16)
    x_buf = x_buf.reshape(expert_devs, local_experts, slot_count, feature_dim)
    g_buf = jnp.einsum("tes,td->esd", gate_sel, grad_f32, precision=highest).astype(jnp.bfloat16)
    g_buf = g_buf.reshape(expert_devs, local_experts, slot_count, feature_dim)
    x_recv, g_recv = (
        lax.all_to_all(x_buf, "expert", split_axis=0, concat_axis=2, tiled=True),
        lax.all_to_all(g_buf, "expert", split_axis=0, concat_axis=2, tiled=True),
    )
    xg_all, gg_all = (
        lax.all_gather(x_recv, "dp", axis=0, tiled=True),
        lax.all_gather(g_recv, "dp", axis=0, tiled=True),
    )
    partial_terms, grad_wi, grad_wo = expert_math(xg_all, gg_all, w_in, w_out)
    summed = lax.psum_scatter(
        partial_terms.astype(jnp.bfloat16), "dp", scatter_dimension=0, tiled=True
    ).astype(jnp.float32)
    out_rows = summed[:, 0].astype(jnp.bfloat16)
    in_rows = summed[:, 1].astype(jnp.bfloat16)
    out_back, in_back = (
        lax.all_to_all(out_rows, "expert", split_axis=2, concat_axis=0, tiled=True),
        lax.all_to_all(in_rows, "expert", split_axis=2, concat_axis=0, tiled=True),
    )
    out_f32 = out_back.reshape(expert_total, slot_count, feature_dim).astype(jnp.float32)
    in_f32 = in_back.reshape(expert_total, slot_count, feature_dim).astype(jnp.float32)
    mixed = jnp.einsum("tes,esd->td", gate_sel, out_f32, precision=highest)
    token_grad = jnp.einsum("tes,esd->td", rows_sel, in_f32, precision=highest)
    dot_vals = jnp.einsum("td,esd->tes", grad_f32, out_f32, precision=highest)
    gate_grad = jnp.einsum("tkes,tes->tk", send_picks, dot_vals, precision=highest)
    return (
        mixed.astype(jnp.bfloat16),
        token_grad.astype(jnp.bfloat16),
        gate_grad,
        grad_wi.astype(jnp.bfloat16),
        grad_wo.astype(jnp.bfloat16),
    )


def solution(mesh):
    in_specs = (
        P(("dp", "expert"), None),
        P(("dp", "expert"), None),
        P(("dp", "expert"), None),
        P(),
        P(),
        P("expert", None, "dp"),
        P("expert", "dp", None),
        P(("dp", "expert"), None),
    )
    out_specs = (
        P(("dp", "expert"), None),
        P(("dp", "expert"), None),
        P(("dp", "expert"), None),
        P("expert", None, "dp"),
        P("expert", "dp", None),
    )
    return jax.shard_map(local, mesh=mesh, in_specs=in_specs, out_specs=out_specs, check_vma=False)
```

profile of v0, /device:TPU:1, one launch (start us, length us, event | category | flops | bytes accessed | tf_op | source)
XLA Modules:
  0.0 473.5 jit_solution(17353640763029097142)
XLA Ops:
  9.0 44.3 %all-gather.1 = s32[64,1,128]{2,1,0:T(1,128)S(1)} all-gather(s32[1,1,128]{2,1,0:T(1,128)S(1)} %bitcast.146), channel_id=2, replica_groups=mesh['dp'=4,'expert'=64] {'expert'}, dimensions={0}, use_global_device_ids=true | all-gather | bytes 33280 | tf_op jit(solution)/shard_map/all_gather | solution.py:9
  56.4 2.5 reshape.109
  59.0 2.4 copy.33
  61.4 35.9 %all_to_all.66 = bf16[64,2,2,2048]{3,1,2,0:T(2,128)(2,1)S(1)} all-to-all(bf16[64,2,2,2048]{3,1,2,0:T(2,128)(2,1)S(1)} %copy.33), channel_id=1, replica_groups=mesh['dp'=4,'expert'=64] {'expert'}, dimensions={0} | all-to-all | bytes 2097152 | tf_op jit(solution)/shard_map/all_to_all | solution.py:74
  101.1 2.5 reshape.110
  103.6 2.4 copy.35
  106.0 34.2 %all_to_all.67 = bf16[64,2,2,2048]{3,1,2,0:T(2,128)(2,1)S(1)} all-to-all(bf16[64,2,2,2048]{3,1,2,0:T(2,128)(2,1)S(1)} %copy.35), channel_id=1, replica_groups=mesh['dp'=4,'expert'=64] {'expert'}, dimensions={0} | all-to-all | bytes 2097152 | tf_op jit(solution)/shard_map/all_to_all | solution.py:75
  141.8 4.5 all-gather.5.cloned.1.call-done
  146.3 5.5 %fusion.1 = f32[2,4,128,384]{3,2,1,0:T(8,128)S(1)} fusion(bf16[4,2,128,2048]{3,2,0,1:T(8,128)(2,1)} %all-gather.5.cloned.1.call-done, bf16[2,2048,384]{2,1,0:T(8,128)(2,1)} %param.15), kind=kOutput, calls=%fused_computation.7 | convolution fusion | flops 1610612736 | bytes 8912896 | tf_op jit(solution)/shard_map/gerd,edh->gerh/dot_general | solution.py:24
  153.0 4.3 convert_bitcast_fusion.1
  157.3 42.5 %all-gather.7.cloned.1.call-done = bf16[4,2,128,2048]{3,2,0,1:T(8,128)(2,1)} async-done(((bf16[1,2,128,2048]{3,2,0,1:T(8,128)(2,1)}), bf16[4,2,128,2048]{3,2,0,1:T(8,128)(2,1)}) %all-gather.7.cloned.1.call-update) | async-done | bytes 4194320 | tf_op jit(solution)/shard_map/all_gather | solution.py:79
  199.8 5.2 %fusion.8 = bf16[4,2,128,384]{3,2,0,1:T(8,128)(2,1)S(1)} fusion(f32[2,4,128,384]{3,2,1,0:T(8,128)} %copy-done.9, bf16[4,2,128,2048]{3,2,0,1:T(8,128)(2,1)} %all-gather.7.cloned.1.call-done, bf16[2,384,2048]{2,1,0:T(8,128)(2,1)S(1)} %copy-done), kind=kOutput, calls=%fused_computation.19 | convolution fusion | flops 1614151680 | bytes 9699328 | tf_op jit(solution)/shard_map/gerd,ehd->gerh/dot_general | solution.py:28
  206.0 2.4 convert_bitcast_fusion
  208.4 6.2 %pad_maximum_fusion = bf16[4,2,2,128,2048]{4,3,0,2,1:T(8,128)(2,1)} fusion(bf16[4,1,2,128,2048]{4,3,0,2,1:T(8,128)(2,1)S(1)} %convert_bitcast_fusion, bf16[4,1,2,128,2048]{4,3,0,2,1:T(8,128)(2,1)} %convert_bitcast_fusion.1), kind=kLoop, calls=%fused_computation.1 | loop fusion | flops 4194304 | bytes 16777216 | tf_op jit(solution)/shard_map/stack | solution.py:33
  215.9 164.5 %all-reduce.3.cloned.1.call-done = bf16[4,2,2,128,2048]{4,3,0,2,1:T(8,128)(2,1)} async-done(((bf16[4,2,2,128,2048]{4,3,0,2,1:T(8,128)(2,1)}), bf16[4,2,2,128,2048]{4,3,0,2,1:T(8,128)(2,1)}) %all-reduce.3.cloned.1.call-update) | async-done | bytes 8388624
  384.8 11.0 %all-to-all-start.2 = ((bf16[1,2,128,2048]{3,1,0,2:T(2,128)(2,1)}), bf16[1,2,128,2048]{3,1,0,2:T(2,128)(2,1)S(1)}, u32[]{:S(2)}, u32[]{:S(2)}) async-start(bf16[1,2,128,2048]{3,1,0,2:T(2,128)(2,1)} %copy.37), calls=%async_computation.2 | async-start | bytes 2097152 | tf_op jit(solution)/shard_map/all_to_all | solution.py:88
  397.9 26.1 %all-to-all-done.2 = bf16[1,2,128,2048]{3,1,0,2:T(2,128)(2,1)S(1)} async-done(((bf16[1,2,128,2048]{3,1,0,2:T(2,128)(2,1)}), bf16[1,2,128,2048]{3,1,0,2:T(2,128)(2,1)S(1)}, u32[]{:S(2)}, u32[]{:S(2)}) %all-to-all-start.2) | async-done | bytes 1048608 | tf_op jit(solution)/shard_map/all_to_all | solution.py:88
  423.9 6.5 %all-to-all-start.3 = ((bf16[1,2,128,2048]{3,1,0,2:T(2,128)(2,1)}), bf16[1,2,128,2048]{3,1,0,2:T(2,128)(2,1)}, u32[]{:S(2)}, u32[]{:S(2)}) async-start(bf16[1,2,128,2048]{3,1,0,2:T(2,128)(2,1)} %copy.39), calls=%async_computation.3 | async-start | bytes 2097152 | tf_op jit(solution)/shard_map/all_to_all | solution.py:89
  430.4 6.4 %bitcast_convert_fusion.1 = bf16[2,2048,384]{2,1,0:T(8,128)(2,1)} fusion(bf16[4,2,128,2048]{3,2,0,1:T(8,128)(2,1)} %all-gather.5.cloned.1.call-done, bf16[4,2,128,384]{3,2,0,1:T(8,128)(2,1)S(1)} %copy-done.4), kind=kOutput, calls=%fused_computation.3 | convolution fusion | flops 1612185600 | bytes 8126464 | tf_op jit(solution)/shard_map/gerd,gerh->edh/dot_general | solution.py:31
  436.8 3.6 bitcast_convert_fusion
  444.1 2.4 fusion.6
  446.5 11.9 %all-to-all-done.3 = bf16[1,2,128,2048]{3,1,0,2:T(2,128)(2,1)} async-done(((bf16[1,2,128,2048]{3,1,0,2:T(2,128)(2,1)}), bf16[1,2,128,2048]{3,1,0,2:T(2,128)(2,1)}, u32[]{:S(2)}, u32[]{:S(2)}) %all-to-all-start.3) | async-done | bytes 1048608 | tf_op jit(solution)/shard_map/all_to_all | solution.py:89
  458.5 3.0 copy.74
  463.7 2.4 fusion.7
  (56 shorter events, 26.9 us)
Async XLA Ops:
  7.2 145.8 %copy-start = (bf16[2,384,2048]{2,1,0:T(8,128)(2,1)S(1)}, bf16[2,384,2048]{2,1,0:T(8,128)(2,1)}, u32[]{:S(2)}) copy-start(bf16[2,384,2048]{2,1,0:T(8,128)(2,1)} %param.16) | copy-start | bytes 9437188
  7.2 139.1 %all-gather.5.cloned.1.call-start = ((), (), s32[]{:S(2)}) async-start(), calls=%async_computation.4 | async-start | bytes 5242880 | tf_op jit(solution)/shard_map/all_gather | solution.py:78
  61.4 37.3 %copy-start.6 = (f32[16,8]{0,1:T(8,128)S(1)}, f32[16,8]{0,1:T(8,128)}, u32[]{:S(2)}) copy-start(f32[16,8]{0,1:T(8,128)} %param.12) | copy-start | bytes 1540
  61.4 37.6 %copy-start.5 = (bf16[16,2048]{1,0:T(8,128)(2,1)S(1)}, bf16[16,2048]{1,0:T(8,128)(2,1)}, u32[]{:S(2)}) copy-start(bf16[16,2048]{1,0:T(8,128)(2,1)} %param.17) | copy-start | bytes 196612
  98.7 101.2 %all-gather.7.cloned.1.call-start = ((), (), s32[]{:S(2)}) async-start(), calls=%async_computation.5 | async-start | bytes 5242880 | tf_op jit(solution)/shard_map/all_gather | solution.py:79
  141.6 238.8 %all-reduce.3.cloned.1.call-start = ((), (), s32[]{:S(2)}) async-start(), calls=%async_computation.6 | async-start | bytes 16777216
  151.8 1.1 copy-start.9
  199.8 6.2 %copy-start.2 = (bf16[2,2048,384]{2,1,0:T(8,128)(2,1)S(1)}, bf16[2,2048,384]{2,1,0:T(8,128)(2,1)}, u32[]{:S(2)}) copy-start(bf16[2,2048,384]{2,1,0:T(8,128)(2,1)} %param.15) | copy-start | bytes 9437188
  205.1 0.9 copy-start.3
  214.6 0.7 copy-start.8
  384.8 45.6 %copy-start.4 = (bf16[4,2,128,384]{3,2,0,1:T(8,128)(2,1)S(1)}, bf16[4,2,128,384]{3,2,0,1:T(8,128)(2,1)}, u32[]{:S(2)}) copy-start(bf16[4,2,128,384]{3,2,0,1:T(8,128)(2,1)} %copy-done.3) | copy-start | bytes 2359300
  384.8 39.2 %all-to-all-start.2 = ((bf16[1,2,128,2048]{3,1,0,2:T(2,128)(2,1)}), bf16[1,2,128,2048]{3,1,0,2:T(2,128)(2,1)S(1)}, u32[]{:S(2)}, u32[]{:S(2)}) async-start(bf16[1,2,128,2048]{3,1,0,2:T(2,128)(2,1)} %copy.37), calls=%async_computation.2 | async-start | bytes 2097152 | tf_op jit(solution)/shard_map/all_to_all | solution.py:88
  423.9 34.6 %all-to-all-start.3 = ((bf16[1,2,128,2048]{3,1,0,2:T(2,128)(2,1)}), bf16[1,2,128,2048]{3,1,0,2:T(2,128)(2,1)}, u32[]{:S(2)}, u32[]{:S(2)}) async-start(bf16[1,2,128,2048]{3,1,0,2:T(2,128)(2,1)} %copy.39), calls=%async_computation.3 | async-start | bytes 2097152 | tf_op jit(solution)/shard_map/all_to_all | solution.py:89
  430.4 6.4 %copy-start.7 = (bf16[4,2,128,2048]{3,2,0,1:T(8,128)(2,1)S(1)}, bf16[4,2,128,2048]{3,2,0,1:T(8,128)(2,1)}, u32[]{:S(2)}) copy-start(bf16[4,2,128,2048]{3,2,0,1:T(8,128)(2,1)} %all-gather.7.cloned.1.call-done) | copy-start | bytes 12582916
  430.4 6.4 %copy-start.10 = (f32[2,4,128,384]{3,2,1,0:T(8,128)S(1)}, f32[2,4,128,384]{3,2,1,0:T(8,128)}, u32[]{:S(2)}) copy-start(f32[2,4,128,384]{3,2,1,0:T(8,128)} %copy-done.9) | copy-start | bytes 4718596
  442.4 24.6 %copy-start.1 = (bf16[2,384,2048]{2,1,0:T(8,128)(2,1)S(1)}, bf16[2,384,2048]{2,1,0:T(8,128)(2,1)}, u32[]{:S(2)}) copy-start(bf16[2,384,2048]{2,1,0:T(8,128)(2,1)} %param.16) | copy-start | bytes 9437188
Sparse Core Ops, SparseCore 0:
  98.8 47.4 all-gather.4
  148.7 51.0 all-gather.6
  214.7 165.5 all-reduce.2
where the time goes:
time: 474 us; the launch traced here: 473 us
  waiting for transfers between devices  250 us (53%)
  blocking collectives  114 us (24%)
  matrix products  38.7 us (8%)
  local copies, waits for them, and re-layouts  31 us (7%)
  starting transfers between devices  17.7 us (4%)
  between operations  14 us (3%)
  other arithmetic  8.05 us (2%)
    unnamed x4, waiting for transfers between devices  165 us
    all_gather x1, blocking collectives, prefix(): gathered = lax.all_gather(part, axis)  44.3 us
    all_gather x1, waiting for transfers between devices, local(): lax.all_gather(g_recv, 'dp', axis=0, tiled=True)  42.5 us
    all_to_all x1, blocking collectives, local(): lax.all_to_all(x_buf, 'expert', split_axis=0, concat_axis=2, tiled=True)  35.9 us
    all_to_all x1, blocking collectives, local(): lax.all_to_all(g_buf, 'expert', split_axis=0, concat_axis=2, tiled=True)  34.2 us
    all_to_all x1, waiting for transfers between devices, local(): lax.all_to_all(out_rows, 'expert', split_axis=2, concat_axis=0, tiled=True)  26.1 us
    all_to_all x1, waiting for transfers between devices, local(): lax.all_to_all(in_rows, 'expert', split_axis=2, concat_axis=0, tiled=True)  11.9 us
    all_to_all x1, starting transfers between devices, local(): lax.all_to_all(out_rows, 'expert', split_axis=2, concat_axis=0, tiled=True)  11 us
  transfers between devices with their start and end apart: 5, of which 5 were waited for; matrix products, arithmetic and copies ran while one was open for 8% of the time, Pallas kernels for 0%

commit v1 on v0

--- a/solution.py
+++ b/solution.py
@@ -2,6 +2,19 @@
 import jax.numpy as jnp
 from jax import lax
 from jax.sharding import PartitionSpec as P
+
+
+def ring_gather(array, axis, dim):
+    ways = lax.axis_size(axis)
+    up = [(d, (d + 1) % ways) for d in range(ways)]
+    down = [(d, (d - 1) % ways) for d in range(ways)]
+    earlier, later = ([array], [array])
+    for _ in range(ways // 2):
+        earlier.append(lax.ppermute(earlier[-1], axis, up))
+    for _ in range((ways - 1) // 2):
+        later.append(lax.ppermute(later[-1], axis, down))
+    line = jnp.concatenate([*earlier[::-1], *later[1:]], axis=dim)
+    return jnp.roll(line, (lax.axis_index(axis) - ways // 2) * array.shape[dim], axis=dim)
 
 
 def prefix(part, axis, combine, identity):
@@ -76,7 +89,7 @@
     )
     xg_all, gg_all = (
         lax.all_gather(x_recv, "dp", axis=0, tiled=True),
-        lax.all_gather(g_recv, "dp", axis=0, tiled=True),
+        ring_gather(g_recv, "dp", 0),
     )
     partial_terms, grad_wi, grad_wo = expert_math(xg_all, gg_all, w_in, w_out)
     summed = lax.psum_scatter(

time: 474 us -> 508 us (1.072)
  blocking collectives: 114 us -> 44.3 us
  waiting for transfers between devices: 250 us -> 311 us
  local copies, waits for them, and re-layouts: 31 us -> 55.4 us
  starting transfers between devices: 17.7 us -> 35.7 us
    all_to_all x2 -> x0, blocking collectives: 70.1 us -> none  [the longest x1 35.9 us: local(): lax.all_to_all(x_buf, 'expert', split_axis=0, concat_axis=2, tiled=True)]
    ppermute x0 -> x3, waiting for transfers between devices: none -> 67.7 us  [the longest x2 67.7 us: ring_gather(): earlier.append(lax.ppermute(earlier[-1], axis, up))]
    all_to_all x0 -> x2, waiting for transfers between devices: none -> 45.2 us  [the longest x1 25.4 us: local(): lax.all_to_all(g_buf, 'expert', split_axis=0, concat_axis=2, tiled=True)]
    all_gather x1 -> x0, waiting for transfers between devices: 42.5 us -> none  [local(): lax.all_gather(g_recv, 'dp', axis=0, tiled=True)]
    unnamed x25 -> x30, local copies, waits for them, and re-layouts: 4.19 us -> 19.7 us
    all_to_all x0 -> x2, starting transfers between devices: none -> 14.4 us  [the longest x1 7.97 us: local(): lax.all_to_all(x_buf, 'expert', split_axis=0, concat_axis=2, tiled=True)]
    unnamed x4 -> x3, waiting for transfers between devices: 165 us -> 162 us
  transfers between devices with their start and end apart: 5 -> 9, of which waited for: 5 -> 7; matrix products, arithmetic and copies ran while one was open for 8% -> 11% of each run, Pallas kernels for 0% -> 0%
where the time goes in v1:
time: 508 us; the launch traced here: 507 us
  waiting for transfers between devices  311 us (61%)
  local copies, waits for them, and re-layouts  55.4 us (11%)
  blocking collectives  44.3 us (9%)
  matrix products  38.6 us (8%)
  starting transfers between devices  35.7 us (7%)
  between operations  14.3 us (3%)
  other arithmetic  8.05 us (2%)
    unnamed x3, waiting for transfers between devices  162 us
    ppermute x2, waiting for transfers between devices, ring_gather(): earlier.append(lax.ppermute(earlier[-1], axis, up))  67.7 us
    all_gather x1, blocking collectives, prefix(): gathered = lax.all_gather(part, axis)  44.3 us
    all_to_all x1, waiting for transfers between devices, local(): lax.all_to_all(out_rows, 'expert', split_axis=2, concat_axis=0, tiled=True)  26.1 us
    all_to_all x1, waiting for transfers between devices, local(): lax.all_to_all(g_buf, 'expert', split_axis=0, concat_axis=2, tiled=True)  25.4 us
    all_to_all x1, waiting for transfers between devices, local(): lax.all_to_all(x_buf, 'expert', split_axis=0, concat_axis=2, tiled=True)  19.8 us
    unnamed x30, local copies, waits for them, and re-layouts  19.7 us
    all_to_all x1, starting transfers between devices, local(): lax.all_to_all(out_rows, 'expert', split_axis=2, concat_axis=0, tiled=True)  10.9 us
  transfers between devices with their start and end apart: 9, of which 7 were waited for; matrix products, arithmetic and copies ran while one was open for 11% of the time, Pallas kernels for 0%

profile of v1, /device:TPU:1, one launch (start us, length us, event | category | flops | bytes accessed | tf_op | source)
XLA Modules:
  0.0 507.1 jit_solution(16171132596820194579)
XLA Ops:
  9.1 44.3 %all-gather.1 = s32[64,1,128]{2,1,0:T(1,128)S(1)} all-gather(s32[1,1,128]{2,1,0:T(1,128)S(1)} %bitcast.142), channel_id=2, replica_groups=mesh['dp'=4,'expert'=64] {'expert'}, dimensions={0}, use_global_device_ids=true | all-gather | bytes 33280 | tf_op jit(solution)/shard_map/all_gather | solution.py:22
  59.0 3.4 copy.33
  62.4 8.0 %all-to-all-start = ((bf16[64,2,2,2048]{3,1,2,0:T(2,128)(2,1)}), bf16[64,2,2,2048]{3,1,2,0:T(2,128)(2,1)}, u32[]{:S(2)}, u32[]{:S(2)}) async-start(bf16[64,2,2,2048]{3,1,2,0:T(2,128)(2,1)} %copy.33), calls=%async_computation | async-start | bytes 2097152 | tf_op jit(solution)/shard_map/all_to_all | solution.py:87
  75.3 3.4 copy.35
  78.7 19.8 %all-to-all-done = bf16[64,2,2,2048]{3,1,2,0:T(2,128)(2,1)} async-done(((bf16[64,2,2,2048]{3,1,2,0:T(2,128)(2,1)}), bf16[64,2,2,2048]{3,1,2,0:T(2,128)(2,1)}, u32[]{:S(2)}, u32[]{:S(2)}) %all-to-all-start) | async-done | bytes 1048608 | tf_op jit(solution)/shard_map/all_to_all | solution.py:87
  98.5 6.5 %all-to-all-start.1 = ((bf16[64,2,2,2048]{3,1,2,0:T(2,128)(2,1)}), bf16[64,2,2,2048]{3,1,2,0:T(2,128)(2,1)}, u32[]{:S(2)}, u32[]{:S(2)}) async-start(bf16[64,2,2,2048]{3,1,2,0:T(2,128)(2,1)} %copy.35), calls=%async_computation.1 | async-start | bytes 2097152 | tf_op jit(solution)/shard_map/all_to_all | solution.py:88
  105.0 2.5 copy.54
  107.6 25.4 %all-to-all-done.1 = bf16[64,2,2,2048]{3,1,2,0:T(2,128)(2,1)} async-done(((bf16[64,2,2,2048]{3,1,2,0:T(2,128)(2,1)}), bf16[64,2,2,2048]{3,1,2,0:T(2,128)(2,1)}, u32[]{:S(2)}, u32[]{:S(2)}) %all-to-all-start.1) | async-done | bytes 1048608 | tf_op jit(solution)/shard_map/all_to_all | solution.py:88
  136.8 45.1 %collective-permute-done = bf16[1,2,128,2048]{3,2,0,1:T(8,128)(2,1)} collective-permute-done((bf16[1,2,128,2048]{3,2,0,1:T(8,128)(2,1)}, bf16[1,2,128,2048]{3,2,0,1:T(8,128)(2,1)}, u32[]{:S(2)}, u32[]{:S(2)}) %collective-permute-start) | collective-permute-done | bytes 1048608 | tf_op jit(solution)/shard_map/ppermute | solution.py:13
  181.9 2.7 collective-permute-start.2
  184.5 22.7 %collective-permute-done.1 = bf16[1,2,128,2048]{3,2,0,1:T(8,128)(2,1)} collective-permute-done((bf16[1,2,128,2048]{3,2,0,1:T(8,128)(2,1)}, bf16[1,2,128,2048]{3,2,0,1:T(8,128)(2,1)}, u32[]{:S(2)}, u32[]{:S(2)}) %collective-permute-start.1) | collective-permute-done | bytes 1048608 | tf_op jit(solution)/shard_map/ppermute | solution.py:13
  211.8 2.6 constant_dynamic-update-slice_fusion.5
  226.1 5.5 %fusion.4 = f32[2,4,128,384]{3,2,1,0:T(8,128)S(1)} fusion(bf16[4,2,128,2048]{3,2,0,1:T(8,128)(2,1)} %all-gather.4.cloned.1.call-done, bf16[2,2048,384]{2,1,0:T(8,128)(2,1)} %param.15), kind=kOutput, calls=%fused_computation.10 | convolution fusion | flops 1610612736 | bytes 8912896 | tf_op jit(solution)/shard_map/gerd,edh->gerh/dot_general | solution.py:37
  231.6 4.4 convert_bitcast_fusion.1
  236.0 4.8 fusion.10
  244.2 6.2 %pad_maximum_fusion = bf16[4,2,2,128,2048]{4,3,0,2,1:T(8,128)(2,1)} fusion(bf16[4,1,2,128,2048]{4,3,0,2,1:T(8,128)(2,1)S(1)} %convert_bitcast_fusion, bf16[4,1,2,128,2048]{4,3,0,2,1:T(8,128)(2,1)} %convert_bitcast_fusion.1), kind=kLoop, calls=%fused_computation.1 | loop fusion | flops 4194304 | bytes 16777216 | tf_op jit(solution)/shard_map/stack | solution.py:46
  251.6 162.2 %all-reduce.3.cloned.1.call-done = bf16[4,2,2,128,2048]{4,3,0,2,1:T(8,128)(2,1)} async-done(((bf16[4,2,2,128,2048]{4,3,0,2,1:T(8,128)(2,1)}), bf16[4,2,2,128,2048]{4,3,0,2,1:T(8,128)(2,1)}) %all-reduce.3.cloned.1.call-update) | async-done | bytes 8388624
  418.2 10.9 %all-to-all-start.2 = ((bf16[1,2,128,2048]{3,1,0,2:T(2,128)(2,1)}), bf16[1,2,128,2048]{3,1,0,2:T(2,128)(2,1)S(1)}, u32[]{:S(2)}, u32[]{:S(2)}) async-start(bf16[1,2,128,2048]{3,1,0,2:T(2,128)(2,1)} %copy.37), calls=%async_computation.2 | async-start | bytes 2097152 | tf_op jit(solution)/shard_map/all_to_all | solution.py:101
  431.2 26.1 %all-to-all-done.2 = bf16[1,2,128,2048]{3,1,0,2:T(2,128)(2,1)S(1)} async-done(((bf16[1,2,128,2048]{3,1,0,2:T(2,128)(2,1)}), bf16[1,2,128,2048]{3,1,0,2:T(2,128)(2,1)S(1)}, u32[]{:S(2)}, u32[]{:S(2)}) %all-to-all-start.2) | async-done | bytes 1048608 | tf_op jit(solution)/shard_map/all_to_all | solution.py:101
  457.3 6.5 %all-to-all-start.3 = ((bf16[1,2,128,2048]{3,1,0,2:T(2,128)(2,1)}), bf16[1,2,128,2048]{3,1,0,2:T(2,128)(2,1)}, u32[]{:S(2)}, u32[]{:S(2)}) async-start(bf16[1,2,128,2048]{3,1,0,2:T(2,128)(2,1)} %copy.39), calls=%async_computation.3 | async-start | bytes 2097152 | tf_op jit(solution)/shard_map/all_to_all | solution.py:102
  463.8 6.4 %bitcast_convert_fusion = bf16[2,384,2048]{2,1,0:T(8,128)(2,1)} fusion(bf16[8,2,128,2048]{3,2,0,1:T(8,128)(2,1)} %constant_dynamic-update-slice_fusion, s32[]{:T(128)S(6)} %select_n.18, f32[2,4,128,384]{3,2,1,0:T(8,128)} %copy-done.9), kind=kOutput, calls=%fused_computation.2 | convolution fusion | flops 1614151680 | bytes 8912900 | tf_op jit(solution)/shard_map/gerh,gerd->ehd/dot_general | solution.py:45
  470.1 4.1 bitcast_convert_fusion.1
  482.3 9.5 %all-to-all-done.3 = bf16[1,2,128,2048]{3,1,0,2:T(2,128)(2,1)} async-done(((bf16[1,2,128,2048]{3,1,0,2:T(2,128)(2,1)}), bf16[1,2,128,2048]{3,1,0,2:T(2,128)(2,1)}, u32[]{:S(2)}, u32[]{:S(2)}) %all-to-all-start.3) | async-done | bytes 1048608 | tf_op jit(solution)/shard_map/all_to_all | solution.py:102
  491.8 2.9 copy.76
  (67 shorter events, 57.2 us)
Async XLA Ops:
  7.2 224.5 %copy-start = (bf16[2,384,2048]{2,1,0:T(8,128)(2,1)S(1)}, bf16[2,384,2048]{2,1,0:T(8,128)(2,1)}, u32[]{:S(2)}) copy-start(bf16[2,384,2048]{2,1,0:T(8,128)(2,1)} %param.16) | copy-start | bytes 9437188
  7.2 63.2 %copy-start.6 = (f32[16,8]{0,1:T(8,128)S(1)}, f32[16,8]{0,1:T(8,128)}, u32[]{:S(2)}) copy-start(f32[16,8]{0,1:T(8,128)} %param.12) | copy-start | bytes 1540
  7.2 63.6 %copy-start.5 = (bf16[16,2048]{1,0:T(8,128)(2,1)S(1)}, bf16[16,2048]{1,0:T(8,128)(2,1)}, u32[]{:S(2)}) copy-start(bf16[16,2048]{1,0:T(8,128)(2,1)} %param.17) | copy-start | bytes 196612
  62.4 36.1 %all-to-all-start = ((bf16[64,2,2,2048]{3,1,2,0:T(2,128)(2,1)}), bf16[64,2,2,2048]{3,1,2,0:T(2,128)(2,1)}, u32[]{:S(2)}, u32[]{:S(2)}) async-start(bf16[64,2,2,2048]{3,1,2,0:T(2,128)(2,1)} %copy.33), calls=%async_computation | async-start | bytes 2097152 | tf_op jit(solution)/shard_map/all_to_all | solution.py:87
  98.5 34.6 %all-to-all-start.1 = ((bf16[64,2,2,2048]{3,1,2,0:T(2,128)(2,1)}), bf16[64,2,2,2048]{3,1,2,0:T(2,128)(2,1)}, u32[]{:S(2)}, u32[]{:S(2)}) async-start(bf16[64,2,2,2048]{3,1,2,0:T(2,128)(2,1)} %copy.35), calls=%async_computation.1 | async-start | bytes 2097152 | tf_op jit(solution)/shard_map/all_to_all | solution.py:88
  105.0 121.1 %all-gather.4.cloned.1.call-start = ((), (), s32[]{:S(2)}) async-start(), calls=%async_computation.4 | async-start | bytes 5242880 | tf_op jit(solution)/shard_map/all_gather | solution.py:91
  107.6 306.3 %all-reduce.3.cloned.1.call-start = ((), (), s32[]{:S(2)}) async-start(), calls=%async_computation.5 | async-start | bytes 16777216
  135.6 46.3 %collective-permute-start = (bf16[1,2,128,2048]{3,2,0,1:T(8,128)(2,1)}, bf16[1,2,128,2048]{3,2,0,1:T(8,128)(2,1)}, u32[]{:S(2)}, u32[]{:S(2)}) collective-permute-start(bf16[1,2,128,2048]{3,2,0,1:T(8,128)(2,1)} %copy.55), channel_id=1, source_target_pairs={{0,64},{64,128},{128,192},{192,0},{1,65},{65,129},{129,193},{193,1... | collective-permute-start | bytes 3145736 | tf_op jit(solution)/shard_map/ppermute | solution.py:13
  181.9 25.4 %collective-permute-start.1 = (bf16[1,2,128,2048]{3,2,0,1:T(8,128)(2,1)}, bf16[1,2,128,2048]{3,2,0,1:T(8,128)(2,1)}, u32[]{:S(2)}, u32[]{:S(2)}) collective-permute-start(bf16[1,2,128,2048]{3,2,0,1:T(8,128)(2,1)} %collective-permute-done), channel_id=1, source_target_pairs={{0,64},{64,128},{128,192},{192,0},{1,65},{65,129},{129,193},{193,1... | collective-permute-start | bytes 3145736 | tf_op jit(solution)/shard_map/ppermute | solution.py:13
  181.9 32.5 %collective-permute-start.2 = (bf16[1,2,128,2048]{3,2,0,1:T(8,128)(2,1)}, bf16[1,2,128,2048]{3,2,0,1:T(8,128)(2,1)}, u32[]{:S(2)}, u32[]{:S(2)}) collective-permute-start(bf16[1,2,128,2048]{3,2,0,1:T(8,128)(2,1)} %copy.55), channel_id=1, source_target_pairs={{0,192},{64,0},{128,64},{192,128},{1,193},{65,1},{129,65},{193,129... | collective-permute-start | bytes 3145736 | tf_op jit(solution)/shard_map/ppermute | solution.py:15
  231.6 4.4 copy-start.9
  236.0 5.8 %copy-start.2 = (bf16[2,2048,384]{2,1,0:T(8,128)(2,1)S(1)}, bf16[2,2048,384]{2,1,0:T(8,128)(2,1)}, u32[]{:S(2)}) copy-start(bf16[2,2048,384]{2,1,0:T(8,128)(2,1)} %param.15) | copy-start | bytes 9437188
  240.8 1.0 copy-start.3
  250.3 0.7 copy-start.8
  418.2 39.0 %all-to-all-start.2 = ((bf16[1,2,128,2048]{3,1,0,2:T(2,128)(2,1)}), bf16[1,2,128,2048]{3,1,0,2:T(2,128)(2,1)S(1)}, u32[]{:S(2)}, u32[]{:S(2)}) async-start(bf16[1,2,128,2048]{3,1,0,2:T(2,128)(2,1)} %copy.37), calls=%async_computation.2 | async-start | bytes 2097152 | tf_op jit(solution)/shard_map/all_to_all | solution.py:101
  457.3 34.5 %all-to-all-start.3 = ((bf16[1,2,128,2048]{3,1,0,2:T(2,128)(2,1)}), bf16[1,2,128,2048]{3,1,0,2:T(2,128)(2,1)}, u32[]{:S(2)}, u32[]{:S(2)}) async-start(bf16[1,2,128,2048]{3,1,0,2:T(2,128)(2,1)} %copy.39), calls=%async_computation.3 | async-start | bytes 2097152 | tf_op jit(solution)/shard_map/all_to_all | solution.py:102
  463.7 6.4 %copy-start.4 = (bf16[4,2,128,384]{3,2,0,1:T(8,128)(2,1)S(1)}, bf16[4,2,128,384]{3,2,0,1:T(8,128)(2,1)}, u32[]{:S(2)}) copy-start(bf16[4,2,128,384]{3,2,0,1:T(8,128)(2,1)} %copy-done.3) | copy-start | bytes 2359300
  463.7 6.4 %copy-start.7 = (bf16[4,2,128,2048]{3,2,0,1:T(8,128)(2,1)S(1)}, bf16[4,2,128,2048]{3,2,0,1:T(8,128)(2,1)}, u32[]{:S(2)}) copy-start(bf16[4,2,128,2048]{3,2,0,1:T(8,128)(2,1)} %all-gather.4.cloned.1.call-done) | copy-start | bytes 12582916
  475.9 24.4 %copy-start.1 = (bf16[2,384,2048]{2,1,0:T(8,128)(2,1)S(1)}, bf16[2,384,2048]{2,1,0:T(8,128)(2,1)}, u32[]{:S(2)}) copy-start(bf16[2,384,2048]{2,1,0:T(8,128)(2,1)} %param.16) | copy-start | bytes 9437188
Sparse Core Ops, SparseCore 0:
  108.2 70.5 all-gather.3
  250.5 163.3 all-reduce.2
